TPU v7x, 512 devices: a whole 4x8x8 slice. The times are simulated.
512 devices in a mesh: pipe: 4 (over z_hi), ctx: 32 (over y, z_lo, core), dp: 4 (over x).
Axes of the slice: x: 4, y: 8, z: 8 (z_hi: 4, z_lo: 2; z = z_hi * 2 + z_lo), core: 2. Of those that a mesh axis runs over, the one named last changes fastest.
Arguments:
- queries: bfloat16 [4, 4, 4096, 4096], P('pipe', 'dp', 'ctx'), may hold values from -7 to 7
- key_input: bfloat16 [4, 4, 4096, 512], P('pipe', 'dp', 'ctx'), may hold values from -4 to 4
- value_input: bfloat16 [4, 4, 4096, 512], P('pipe', 'dp', 'ctx'), may hold values from -6 to 6
- incoming: bfloat16 [4, 4, 4096, 4096], P('pipe', 'dp', 'ctx'), may hold values from -6 to 6
- segments: int32 [4, 4096], P('dp'), may hold values from 0 to 15, never falling along the last dimension, each value on 1 to 512 neighbouring positions
Outputs:
- query_grad: bfloat16 [4, 4, 4096, 4096], P('pipe', 'dp', 'ctx')
- key_grad: bfloat16 [4, 4, 4096, 512], P('pipe', 'dp', 'ctx')
- value_grad: bfloat16 [4, 4, 4096, 512], P('pipe', 'dp', 'ctx')
- bias_grad: float32 [4, 5120], P('pipe')
Inputs may be any that keep to these rules, and one draw needn't show every extreme that they name: `segments`: tokens of one document are contiguous; every document holds 1 to 512 tokens and one holds exactly 512.
All inputs are finite; a program needn't handle non-finite values.
Results may differ from a plain program's by a relative error of at most 0.009.
Values may be sent and summed in bfloat16 or wider, within the bound.
No kernel may reach another device: no remote copies, remote signals or barrier semaphores. Data moves between devices by JAX's collectives and lax.ppermute only.
A program may use at most 64 MiB of HBM per device.

v0:
```python
import math
import jax
import jax.numpy as jnp
from jax import lax
from jax.sharding import PartitionSpec as P

ASKER_STREAMS = 32
SHARED_GROUPS = 4
FEATURE_SIZE = 128
QUERY_PER_KEY = 8


def passed_along(value, axis, steps):
    count = lax.axis_size(axis)
    pairs = [(source, (source + steps) % count) for source in range(count)]
    return lax.ppermute(value, axis, pairs)


def attend(
    queries, key_rows, value_rows, cotangent, query_doc, key_doc, query_pos, key_pos, scaling
):
    scores = (
        jnp.einsum("gqd,kd->gqk", queries, key_rows, preferred_element_type=jnp.float32) * scaling
    )
    visible = (query_doc[:, None] == key_doc[None, :]) & (key_pos[None, :] <= query_pos[:, None])
    scores = jnp.where(visible[None], scores, -1e30)
    row_max = jnp.max(scores, axis=-1, keepdims=True)
    weights = jnp.where(visible[None], jnp.exp(scores - row_max), 0.0)
    probs = weights / jnp.sum(weights, axis=-1, keepdims=True)
    probs_b = probs.astype(jnp.bfloat16)
    attn_out = jnp.einsum("gqk,kd->gqd", probs_b, value_rows, preferred_element_type=jnp.float32)
    dot_out = jnp.sum(cotangent.astype(jnp.float32) * attn_out, axis=-1, keepdims=True)
    grad_prob = jnp.einsum("gqd,kd->gqk", cotangent, value_rows, preferred_element_type=jnp.float32)
    grad_score = (probs * (grad_prob - dot_out) * scaling).astype(jnp.bfloat16)
    asker_derivative = jnp.einsum(
        "gqk,kd->gqd", grad_score, key_rows, preferred_element_type=jnp.float32
    )
    lookup_derivative = jnp.einsum(
        "gqk,gqd->kd", grad_score, queries, preferred_element_type=jnp.float32
    )
    content_derivative = jnp.einsum(
        "gqk,gqd->kd", probs_b, cotangent, preferred_element_type=jnp.float32
    )
    return (asker_derivative, lookup_derivative, content_derivative)


def banded(queries, key_rows, value_rows, cotangent, doc_ids, block_len, scaling):
    length = doc_ids.shape[0]
    blocks = length // block_len
    width = key_rows.shape[1]
    key_pad = jnp.concatenate([jnp.zeros((block_len, width), key_rows.dtype), key_rows], axis=0)
    value_pad = jnp.concatenate(
        [jnp.zeros((block_len, width), value_rows.dtype), value_rows], axis=0
    )
    doc_pad = jnp.concatenate([jnp.full((block_len,), -1, jnp.int32), doc_ids])
    pos_pad = jnp.arange(length + block_len, dtype=jnp.int32) - block_len

    def step(carried, block):
        key_acc, value_acc = carried
        anchor = block * block_len
        query_blk = lax.dynamic_slice_in_dim(queries, anchor, block_len, 1)
        cot_blk = lax.dynamic_slice_in_dim(cotangent, anchor, block_len, 1)
        key_blk = lax.dynamic_slice_in_dim(key_pad, anchor, 2 * block_len, 0)
        value_blk = lax.dynamic_slice_in_dim(value_pad, anchor, 2 * block_len, 0)
        query_doc = lax.dynamic_slice_in_dim(doc_ids, anchor, block_len, 0)
        key_doc = lax.dynamic_slice_in_dim(doc_pad, anchor, 2 * block_len, 0)
        query_pos = anchor + jnp.arange(block_len, dtype=jnp.int32)
        key_pos = lax.dynamic_slice_in_dim(pos_pad, anchor, 2 * block_len, 0)
        asker_derivative, lookup_derivative, content_derivative = attend(
            query_blk, key_blk, value_blk, cot_blk, query_doc, key_doc, query_pos, key_pos, scaling
        )
        key_acc = lax.dynamic_update_slice_in_dim(
            key_acc,
            lax.dynamic_slice_in_dim(key_acc, anchor, 2 * block_len, 0) + lookup_derivative,
            anchor,
            0,
        )
        value_acc = lax.dynamic_update_slice_in_dim(
            value_acc,
            lax.dynamic_slice_in_dim(value_acc, anchor, 2 * block_len, 0) + content_derivative,
            anchor,
            0,
        )
        return ((key_acc, value_acc), asker_derivative)

    start_acc = jnp.zeros((length + block_len, width), jnp.float32)
    (key_acc, value_acc), query_blocks = lax.scan(
        step, (start_acc, start_acc), jnp.arange(blocks, dtype=jnp.int32)
    )
    groups = queries.shape[0]
    asker_derivative = query_blocks.transpose(1, 0, 2, 3).reshape(groups, length, width)
    return (asker_derivative, key_acc[block_len:], value_acc[block_len:])


def body(queries, key_input, value_input, incoming, segments):
    shard_length = queries.shape[2]
    ctx_size = lax.axis_size("ctx")
    reach_dev = min(4, ctx_size - 1)
    block_len = reach_dev * shard_length
    scaling = 1.0 / math.sqrt(FEATURE_SIZE)
    doc_ids = segments[0]
    handed = passed_along(incoming, "pipe", -1)
    query_tok = queries[0, 0].reshape(shard_length, ASKER_STREAMS, FEATURE_SIZE)
    cot_tok = handed[0, 0].reshape(shard_length, ASKER_STREAMS, FEATURE_SIZE)
    key_widened = jnp.repeat(
        key_input[0, 0].reshape(shard_length, SHARED_GROUPS, FEATURE_SIZE), QUERY_PER_KEY, axis=1
    )
    value_widened = jnp.repeat(
        value_input[0, 0].reshape(shard_length, SHARED_GROUPS, FEATURE_SIZE), QUERY_PER_KEY, axis=1
    )
    query_head, key_head, value_head, cot_head = (
        lax.all_to_all(query_tok, "ctx", split_axis=1, concat_axis=0, tiled=True),
        lax.all_to_all(key_widened, "ctx", split_axis=1, concat_axis=0, tiled=True),
        lax.all_to_all(value_widened, "ctx", split_axis=1, concat_axis=0, tiled=True),
        lax.all_to_all(cot_tok, "ctx", split_axis=1, concat_axis=0, tiled=True),
    )

    def per_head(members):
        return banded(
            members[0][None], members[1], members[2], members[3][None], doc_ids, block_len, scaling
        )

    asker_derivative, lookup_derivative, content_derivative = lax.map(
        per_head,
        (
            query_head.transpose(1, 0, 2),
            key_head.transpose(1, 0, 2),
            value_head.transpose(1, 0, 2),
            cot_head.transpose(1, 0, 2),
        ),
    )
    asker_derivative = asker_derivative[:, 0].transpose(1, 0, 2)
    lookup_derivative = lookup_derivative.transpose(1, 0, 2)
    content_derivative = content_derivative.transpose(1, 0, 2)
    query_back, key_backward, value_backward = (
        lax.all_to_all(asker_derivative, "ctx", split_axis=0, concat_axis=1, tiled=True),
        lax.all_to_all(lookup_derivative, "ctx", split_axis=0, concat_axis=1, tiled=True),
        lax.all_to_all(content_derivative, "ctx", split_axis=0, concat_axis=1, tiled=True),
    )
    query_flat = query_back.reshape(shard_length, ASKER_STREAMS * FEATURE_SIZE)
    key_flattened = (
        key_backward.reshape(shard_length, SHARED_GROUPS, QUERY_PER_KEY, FEATURE_SIZE)
        .sum(axis=2)
        .reshape(shard_length, SHARED_GROUPS * FEATURE_SIZE)
    )
    value_flat = (
        value_backward.reshape(shard_length, SHARED_GROUPS, QUERY_PER_KEY, FEATURE_SIZE)
        .sum(axis=2)
        .reshape(shard_length, SHARED_GROUPS * FEATURE_SIZE)
    )
    offset_parts = jnp.concatenate(
        [jnp.sum(query_flat, axis=0), jnp.sum(key_flattened, axis=0), jnp.sum(value_flat, axis=0)]
    )
    offset_overall = lax.psum(offset_parts, ("ctx", "dp"))
    bias_scaled = offset_overall / math.sqrt(lax.axis_size("dp") * shard_length * ctx_size)
    query_grad = query_flat.astype(jnp.bfloat16)[None, None]
    key_grad = key_flattened.astype(jnp.bfloat16)[None, None]
    value_grad = value_flat.astype(jnp.bfloat16)[None, None]
    return (query_grad, key_grad, value_grad, bias_scaled[None])


def solution(mesh):
    return jax.shard_map(
        body,
        mesh=mesh,
        in_specs=(
            P("pipe", "dp", "ctx", None),
            P("pipe", "dp", "ctx", None),
            P("pipe", "dp", "ctx", None),
            P("pipe", "dp", "ctx", None),
            P("dp", None),
        ),
        out_specs=(
            P("pipe", "dp", "ctx", None),
            P("pipe", "dp", "ctx", None),
            P("pipe", "dp", "ctx", None),
            P("pipe", None),
        ),
        check_vma=False,
    )
```

profile of v0, /device:TPU:128, one launch (start us, length us, event | category | flops | bytes accessed | tf_op | source)
XLA Modules:
  0.0 1042.6 jit_solution(12610844461914456718)
XLA Ops:
  2.9 9.3 all-to-all-start.1
  12.2 28.5 %all-to-all-done.1 = bf16[128,32,128]{2,0,1:T(8,128)(2,1)S(1)} async-done(((bf16[128,32,128]{2,0,1:T(8,128)(2,1)}), bf16[128,32,128]{2,0,1:T(8,128)(2,1)S(1)}, u32[]{:S(2)}, u32[]{:S(2)}) %all-to-all-start.1) | async-done | bytes 1048608 | tf_op jit(solution)/shard_map/all_to_all | solution.py:113
  42.0 3.9 all-to-all-start.3
  45.9 1.9 collective-permute-start
  47.8 37.3 %collective-permute-done = bf16[1,1,128,4096]{3,2,1,0:T(8,128)(2,1)S(1)} collective-permute-done((bf16[1,1,128,4096]{3,2,1,0:T(8,128)(2,1)}, bf16[1,1,128,4096]{3,2,1,0:T(8,128)(2,1)S(1)}, u32[]{:S(2)}, u32[]{:S(2)}) %collective-permute-start) | collective-permute-done | bytes 1048608 | tf_op jit(solution)/shard_map/ppermute | solution.py:16
  86.5 30.7 %all-to-all-start.2 = ((bf16[128,32,128]{0,2,1:T(8,128)(2,1)}), bf16[128,32,128]{0,2,1:T(8,128)(2,1)S(1)}, u32[]{:S(2)}, u32[]{:S(2)}) async-start(bf16[128,32,128]{0,2,1:T(8,128)(2,1)} %bitcast.112), calls=%async_computation.2 | async-start | bytes 2097152 | tf_op jit(solution)/shard_map/all_to_all | solution.py:115
  120.1 25.7 %all-to-all-done.2 = bf16[128,32,128]{0,2,1:T(8,128)(2,1)S(1)} async-done(((bf16[128,32,128]{0,2,1:T(8,128)(2,1)}), bf16[128,32,128]{0,2,1:T(8,128)(2,1)S(1)}, u32[]{:S(2)}, u32[]{:S(2)}) %all-to-all-start.2) | async-done | bytes 1048608 | tf_op jit(solution)/shard_map/all_to_all | solution.py:115
  145.8 4.7 all-to-all-start
  154.3 25.3 %all-to-all-done = bf16[128,32,128]{2,0,1:T(8,128)(2,1)} async-done(((bf16[128,32,128]{2,0,1:T(8,128)(2,1)}), bf16[128,32,128]{2,0,1:T(8,128)(2,1)}, u32[]{:S(2)}, u32[]{:S(2)}) %all-to-all-start) | async-done | bytes 1048608 | tf_op jit(solution)/shard_map/all_to_all | solution.py:112
  183.3 126.4 %while.25 = (s32[]{:T(128)}, f32[4608,128]{1,0:T(8,128)}, f32[4608,128]{1,0:T(8,128)}, f32[8,1,512,128]{3,2,1,0:T(8,128)}, s32[8]{0:T(128)}, /*index=5*/s32[4096...) while((s32[]{:T(128)}, f32[4608,128]{1,0:T(8,128)}, ...), condition=%wide.region_4.5_spmd, body=%wide.region_0.4_spmd.sunk | while | flops 820444160 | bytes 22487844 | solution.py:87
  192.3 2.4 fusion.59
  194.7 2.1 fusion.61
  196.8 2.3 fusion.60
  208.1 2.4 fusion.59
  210.5 2.1 fusion.61
  212.6 2.3 fusion.60
  218.3 1.7 fusion.55
  223.9 2.4 fusion.59
  226.3 2.1 fusion.61
  228.4 2.3 fusion.60
  234.1 1.7 fusion.55
  239.7 2.4 fusion.59
  242.1 2.1 fusion.61
  244.2 2.3 fusion.60
  249.9 1.7 fusion.55
  255.5 2.4 fusion.59
  257.9 2.1 fusion.61
  260.0 2.3 fusion.60
  265.7 1.7 fusion.55
  271.3 2.4 fusion.59
  273.7 2.1 fusion.61
  275.8 2.3 fusion.60
  287.1 2.4 fusion.59
  289.5 2.1 fusion.61
  291.6 2.3 fusion.60
  302.9 2.4 fusion.59
  305.3 2.1 fusion.61
  307.4 2.3 fusion.60
  309.7 3.1 slice.8
  312.8 4.0 all-to-all-start.5
  316.8 3.1 slice.9
  319.9 48.6 %all-to-all-done.5 = f32[4096,1,128]{2,1,0:T(1,128)S(1)} async-done(((f32[4096,1,128]{2,1,0:T(1,128)}), f32[4096,1,128]{2,1,0:T(1,128)S(1)}, u32[]{:S(2)}, u32[]{:S(2)}) %all-to-all-start.5) | async-done | bytes 2097184 | tf_op jit(solution)/shard_map/all_to_all | solution.py:137
  368.5 56.4 %all_to_all.105 = f32[4096,1,128]{2,1,0:T(1,128)} all-to-all(f32[4096,1,128]{2,1,0:T(1,128)} %bitcast.109), channel_id=1, replica_groups=mesh['pipe'=4,'ctx'=32,'dp'=4] {'ctx'}, dimensions={0} | all-to-all | bytes 4194304 | tf_op jit(solution)/shard_map/all_to_all | solution.py:138
  424.9 4.8 all-to-all-start.4
  431.6 49.7 %all-to-all-done.4 = f32[4096,1,128]{2,1,0:T(1,128)} async-done(((f32[4096,1,128]{2,1,0:T(1,128)}), f32[4096,1,128]{2,1,0:T(1,128)}, u32[]{:S(2)}, u32[]{:S(2)}) %all-to-all-start.4) | async-done | bytes 2097184 | tf_op jit(solution)/shard_map/all_to_all | solution.py:136
  481.3 1.8 convert_element_type.50
  484.8 549.9 %psum.7 = f32[5120]{0:T(1024)S(1)} all-reduce(f32[5120]{0:T(1024)S(1)} %pad_maximum_fusion), channel_id=1, replica_groups=mesh['pipe'=4,'ctx'=32,'dp'=4] {'ctx','dp'}, use_global_device_ids=true, to_apply=%region_12.13 | all-reduce | flops 5120 | bytes 40960 | tf_op jit(solution)/shard_map/psum | solution.py:154
  1036.6 2.3 copy.50
  (129 shorter events, 84.4 us)
Async XLA Ops:
  0.6 11.5 %copy-start = (bf16[1,1,128,512]{3,2,1,0:T(8,128)(2,1)S(1)}, bf16[1,1,128,512]{3,2,1,0:T(8,128)(2,1)}, u32[]{:S(2)}) copy-start(bf16[1,1,128,512]{3,2,1,0:T(8,128)(2,1)} %param.9) | copy-start | bytes 393220
  2.9 37.9 %all-to-all-start.1 = ((bf16[128,32,128]{2,0,1:T(8,128)(2,1)}), bf16[128,32,128]{2,0,1:T(8,128)(2,1)S(1)}, u32[]{:S(2)}, u32[]{:S(2)}) async-start(bf16[128,32,128]{2,0,1:T(8,128)(2,1)} %bitcast.9), calls=%async_computation.1 | async-start | bytes 2097152 | tf_op jit(solution)/shard_map/all_to_all | solution.py:113
  42.0 44.5 %all-to-all-start.3 = ((bf16[128,32,128]{2,0,1:T(8,128)(2,1)}), bf16[128,32,128]{2,0,1:T(8,128)(2,1)S(1)}, u32[]{:S(2)}, u32[]{:S(2)}) async-start(bf16[128,32,128]{2,0,1:T(8,128)(2,1)} %bitcast.17), calls=%async_computation.3 | async-start | bytes 2097152 | tf_op jit(solution)/shard_map/all_to_all | solution.py:114
  45.9 39.3 %collective-permute-start = (bf16[1,1,128,4096]{3,2,1,0:T(8,128)(2,1)}, bf16[1,1,128,4096]{3,2,1,0:T(8,128)(2,1)S(1)}, u32[]{:S(2)}, u32[]{:S(2)}) collective-permute-start(bf16[1,1,128,4096]{3,2,1,0:T(8,128)(2,1)} %param.10), channel_id=1, source_target_pairs={{0,384},{128,0},{256,128},{384,256},{1,385},{129,1},{257,129},{385... | collective-permute-start | bytes 3145736 | tf_op jit(solution)/shard_map/ppermute | solution.py:16
  86.5 59.3 %all-to-all-start.2 = ((bf16[128,32,128]{0,2,1:T(8,128)(2,1)}), bf16[128,32,128]{0,2,1:T(8,128)(2,1)S(1)}, u32[]{:S(2)}, u32[]{:S(2)}) async-start(bf16[128,32,128]{0,2,1:T(8,128)(2,1)} %bitcast.112), calls=%async_computation.2 | async-start | bytes 2097152 | tf_op jit(solution)/shard_map/all_to_all | solution.py:115
  118.7 31.8 %copy-start.1 = (s32[1,4096]{1,0:T(1,128)S(1)}, s32[1,4096]{1,0:T(1,128)}, u32[]{:S(2)}) copy-start(s32[1,4096]{1,0:T(1,128)} %param.11) | copy-start | bytes 49156
  145.8 33.8 %all-to-all-start = ((bf16[128,32,128]{2,0,1:T(8,128)(2,1)}), bf16[128,32,128]{2,0,1:T(8,128)(2,1)}, u32[]{:S(2)}, u32[]{:S(2)}) async-start(bf16[128,32,128]{2,0,1:T(8,128)(2,1)} %copy.41), calls=%async_computation | async-start | bytes 2097152 | tf_op jit(solution)/shard_map/all_to_all | solution.py:112
  312.8 55.7 %all-to-all-start.5 = ((f32[4096,1,128]{2,1,0:T(1,128)}), f32[4096,1,128]{2,1,0:T(1,128)S(1)}, u32[]{:S(2)}, u32[]{:S(2)}) async-start(f32[4096,1,128]{2,1,0:T(1,128)} %bitcast.108), calls=%async_computation.5 | async-start | bytes 4194304 | tf_op jit(solution)/shard_map/all_to_all | solution.py:137
  424.9 56.4 %all-to-all-start.4 = ((f32[4096,1,128]{2,1,0:T(1,128)}), f32[4096,1,128]{2,1,0:T(1,128)}, u32[]{:S(2)}, u32[]{:S(2)}) async-start(f32[4096,1,128]{2,1,0:T(1,128)} %bitcast.116), calls=%async_computation.4 | async-start | bytes 4194304 | tf_op jit(solution)/shard_map/all_to_all | solution.py:136
where the time goes:
time: 1050 us; the launch traced here: 1040 us
  blocking collectives  606 us (58%)
  waiting for transfers between devices  215 us (20%)
  matrix products  76.1 us (7%)
  starting transfers between devices  59.3 us (6%)
  local copies, waits for them, and re-layouts  57 us (5%)
  other arithmetic  23 us (2%)
    psum x1, blocking collectives, body(): offset_overall = lax.psum(offset_parts, ('ctx', 'dp'))  550 us
    all_to_all x1, blocking collectives, body(): lax.all_to_all(content_derivative, 'ctx', split_axis=0, concat_axis=1, ti...  56.4 us
    all_to_all x1, waiting for transfers between devices, body(): lax.all_to_all(asker_derivative, 'ctx', split_axis=0, concat_axis=1, tile...  49.7 us
    all_to_all x1, waiting for transfers between devices, body(): lax.all_to_all(lookup_derivative, 'ctx', split_axis=0, concat_axis=1, til...  48.6 us
    ppermute x1, waiting for transfers between devices, passed_along(): return lax.ppermute(value, axis, pairs)  37.3 us
    all_to_all x1, starting transfers between devices, body(): lax.all_to_all(cot_tok, 'ctx', split_axis=1, concat_axis=0, tiled=True)  30.7 us
    all_to_all x1, waiting for transfers between devices, body(): lax.all_to_all(key_widened, 'ctx', split_axis=1, concat_axis=0, tiled=True)  28.5 us
    all_to_all x1, waiting for transfers between devices, body(): lax.all_to_all(cot_tok, 'ctx', split_axis=1, concat_axis=0, tiled=True)  25.7 us
  transfers between devices with their start and end apart: 7, of which 6 were waited for; matrix products, arithmetic and copies ran while one was open for 1% of the time, Pallas kernels for 0%

commit v1 on v0

--- a/solution.py
+++ b/solution.py
@@ -151,7 +151,7 @@
     offset_parts = jnp.concatenate(
         [jnp.sum(query_flat, axis=0), jnp.sum(key_flattened, axis=0), jnp.sum(value_flat, axis=0)]
     )
-    offset_overall = lax.psum(offset_parts, ("ctx", "dp"))
+    offset_overall = jnp.sum(lax.all_gather(offset_parts, ("ctx", "dp")), axis=0)
     bias_scaled = offset_overall / math.sqrt(lax.axis_size("dp") * shard_length * ctx_size)
     query_grad = query_flat.astype(jnp.bfloat16)[None, None]
     key_grad = key_flattened.astype(jnp.bfloat16)[None, None]

time: 1050 us -> 868 us (0.83)
  the two profiles are of different devices: /device:TPU:128 before, /device:TPU:27 now
where the time goes in v1:
time: 868 us; the launch traced here: 865 us
  waiting for transfers between devices  573 us (66%)
  matrix products  76.2 us (9%)
  local copies, waits for them, and re-layouts  59.4 us (7%)
  blocking collectives  57.4 us (7%)
  starting transfers between devices  56.5 us (7%)
  other arithmetic  23.8 us (3%)
  between operations  14.2 us (2%)
    all_gather x1, waiting for transfers between devices, body(): lax.all_gather(offset_parts, ('ctx', 'dp'))  359 us
    all_to_all x1, blocking collectives, body(): lax.all_to_all(content_derivative, 'ctx', split_axis=0, concat_axis=1, ti...  57.4 us
    ppermute x1, waiting for transfers between devices, passed_along(): return lax.ppermute(value, axis, pairs)  53.1 us
    all_to_all x1, waiting for transfers between devices, body(): lax.all_to_all(asker_derivative, 'ctx', split_axis=0, concat_axis=1, tile...  45.4 us
    all_to_all x1, waiting for transfers between devices, body(): lax.all_to_all(lookup_derivative, 'ctx', split_axis=0, concat_axis=1, til...  44.2 us
    all_to_all x1, waiting for transfers between devices, body(): lax.all_to_all(key_widened, 'ctx', split_axis=1, concat_axis=0, tiled=True)  25.7 us
    all_to_all x1, waiting for transfers between devices, body(): lax.all_to_all(cot_tok, 'ctx', split_axis=1, concat_axis=0, tiled=True)  22.9 us
    all_to_all x1, waiting for transfers between devices, body(): lax.all_to_all(query_tok, 'ctx', split_axis=1, concat_axis=0, tiled=True)  22.1 us
  transfers between devices with their start and end apart: 8, of which 7 were waited for; matrix products, arithmetic and copies ran while one was open for 3% of the time, Pallas kernels for 0%

profile of v1, /device:TPU:27, one launch (start us, length us, event | category | flops | bytes accessed | tf_op | source)
XLA Modules:
  0.0 865.0 jit_solution(17443677443313876487)
XLA Ops:
  9.4 9.6 %all-to-all-start.1 = ((bf16[128,32,128]{2,0,1:T(8,128)(2,1)}), bf16[128,32,128]{2,0,1:T(8,128)(2,1)S(1)}, u32[]{:S(2)}, u32[]{:S(2)}) async-start(bf16[128,32,128]{2,0,1:T(8,128)(2,1)} %bitcast.9), calls=%async_computation.1 | async-start | bytes 2097152 | tf_op jit(solution)/shard_map/all_to_all | solution.py:113
  19.0 25.7 %all-to-all-done.1 = bf16[128,32,128]{2,0,1:T(8,128)(2,1)S(1)} async-done(((bf16[128,32,128]{2,0,1:T(8,128)(2,1)}), bf16[128,32,128]{2,0,1:T(8,128)(2,1)S(1)}, u32[]{:S(2)}, u32[]{:S(2)}) %all-to-all-start.1) | async-done | bytes 1048608 | tf_op jit(solution)/shard_map/all_to_all | solution.py:113
  45.9 6.8 all-to-all-start.3
  52.7 9.8 %collective-permute-start = (bf16[1,1,128,4096]{3,2,1,0:T(8,128)(2,1)}, bf16[1,1,128,4096]{3,2,1,0:T(8,128)(2,1)S(1)}, u32[]{:S(2)}, u32[]{:S(2)}) collective-permute-start(bf16[1,1,128,4096]{3,2,1,0:T(8,128)(2,1)} %param.10), channel_id=1, source_target_pairs={{0,384},{128,0},{256,128},{384,256},{1,385},{129,1},{257,129},{385... | collective-permute-start | bytes 3145736 | tf_op jit(solution)/shard_map/ppermute | solution.py:16
  62.4 53.1 %collective-permute-done = bf16[1,1,128,4096]{3,2,1,0:T(8,128)(2,1)S(1)} collective-permute-done((bf16[1,1,128,4096]{3,2,1,0:T(8,128)(2,1)}, bf16[1,1,128,4096]{3,2,1,0:T(8,128)(2,1)S(1)}, u32[]{:S(2)}, u32[]{:S(2)}) %collective-permute-start) | collective-permute-done | bytes 1048608 | tf_op jit(solution)/shard_map/ppermute | solution.py:16
  116.9 7.5 all-to-all-start.2
  127.3 22.9 %all-to-all-done.2 = bf16[128,32,128]{0,2,1:T(8,128)(2,1)S(1)} async-done(((bf16[128,32,128]{0,2,1:T(8,128)(2,1)}), bf16[128,32,128]{0,2,1:T(8,128)(2,1)S(1)}, u32[]{:S(2)}, u32[]{:S(2)}) %all-to-all-start.2) | async-done | bytes 1048608 | tf_op jit(solution)/shard_map/all_to_all | solution.py:115
  150.1 7.4 all-to-all-start
  161.3 22.1 %all-to-all-done = bf16[128,32,128]{2,0,1:T(8,128)(2,1)} async-done(((bf16[128,32,128]{2,0,1:T(8,128)(2,1)}), bf16[128,32,128]{2,0,1:T(8,128)(2,1)}, u32[]{:S(2)}, u32[]{:S(2)}) %all-to-all-start) | async-done | bytes 1048608 | tf_op jit(solution)/shard_map/all_to_all | solution.py:112
  187.0 126.4 %while.25 = (s32[]{:T(128)}, f32[4608,128]{1,0:T(8,128)}, f32[4608,128]{1,0:T(8,128)}, f32[8,1,512,128]{3,2,1,0:T(8,128)}, s32[8]{0:T(128)}, /*index=5*/s32[4096...) while((s32[]{:T(128)}, f32[4608,128]{1,0:T(8,128)}, ...), condition=%wide.region_4.5_spmd, body=%wide.region_0.4_spmd.sunk | while | flops 820444160 | bytes 22487844 | solution.py:87
  190.4 1.7 fusion.55
  196.0 2.4 fusion.59
  198.4 2.1 fusion.61
  200.5 2.3 fusion.60
  211.8 2.4 fusion.59
  214.2 2.1 fusion.61
  216.3 2.3 fusion.60
  222.0 1.8 fusion.55
  227.6 2.4 fusion.59
  230.0 2.1 fusion.61
  232.1 2.3 fusion.60
  237.8 1.8 fusion.55
  243.4 2.4 fusion.59
  245.8 2.1 fusion.61
  247.9 2.3 fusion.60
  259.2 2.4 fusion.59
  261.6 2.1 fusion.61
  263.7 2.3 fusion.60
  275.0 2.4 fusion.59
  277.5 2.1 fusion.61
  279.6 2.3 fusion.60
  290.9 2.4 fusion.59
  293.3 2.1 fusion.61
  295.4 2.3 fusion.60
  306.6 2.4 fusion.59
  309.1 2.1 fusion.61
  311.2 2.3 fusion.60
  313.5 3.1 slice.8
  316.6 7.4 all-to-all-start.5
  324.0 3.1 slice.9
  327.1 44.2 %all-to-all-done.5 = f32[4096,1,128]{2,1,0:T(1,128)S(1)} async-done(((f32[4096,1,128]{2,1,0:T(1,128)}), f32[4096,1,128]{2,1,0:T(1,128)S(1)}, u32[]{:S(2)}, u32[]{:S(2)}) %all-to-all-start.5) | async-done | bytes 2097184 | tf_op jit(solution)/shard_map/all_to_all | solution.py:137
  371.3 57.4 %all_to_all.105 = f32[4096,1,128]{2,1,0:T(1,128)} all-to-all(f32[4096,1,128]{2,1,0:T(1,128)} %bitcast.109), channel_id=1, replica_groups=mesh['pipe'=4,'ctx'=32,'dp'=4] {'ctx'}, dimensions={0} | all-to-all | bytes 4194304 | tf_op jit(solution)/shard_map/all_to_all | solution.py:138
  428.7 8.1 all-to-all-start.4
  438.7 45.4 %all-to-all-done.4 = f32[4096,1,128]{2,1,0:T(1,128)} async-done(((f32[4096,1,128]{2,1,0:T(1,128)}), f32[4096,1,128]{2,1,0:T(1,128)}, u32[]{:S(2)}, u32[]{:S(2)}) %all-to-all-start.4) | async-done | bytes 2097184 | tf_op jit(solution)/shard_map/all_to_all | solution.py:136
  486.4 1.8 convert_element_type.50
  489.5 2.3 copy.50
  495.4 359.4 %all-gather.3.cloned.1.call-done = f32[655360]{0:T(1024)} async-done(((f32[5120]{0:T(1024)}), f32[655360]{0:T(1024)}) %all-gather.3.cloned.1.call-update) | async-done | bytes 2621456 | tf_op jit(solution)/shard_map/all_gather | solution.py:154
  854.9 2.5 reshape.145
  (133 shorter events, 86.8 us)
Async XLA Ops:
  7.2 11.8 %copy-start = (bf16[1,1,128,512]{3,2,1,0:T(8,128)(2,1)S(1)}, bf16[1,1,128,512]{3,2,1,0:T(8,128)(2,1)}, u32[]{:S(2)}) copy-start(bf16[1,1,128,512]{3,2,1,0:T(8,128)(2,1)} %param.9) | copy-start | bytes 393220
  9.4 35.3 %all-to-all-start.1 = ((bf16[128,32,128]{2,0,1:T(8,128)(2,1)}), bf16[128,32,128]{2,0,1:T(8,128)(2,1)S(1)}, u32[]{:S(2)}, u32[]{:S(2)}) async-start(bf16[128,32,128]{2,0,1:T(8,128)(2,1)} %bitcast.9), calls=%async_computation.1 | async-start | bytes 2097152 | tf_op jit(solution)/shard_map/all_to_all | solution.py:113
  45.9 71.0 %all-to-all-start.3 = ((bf16[128,32,128]{2,0,1:T(8,128)(2,1)}), bf16[128,32,128]{2,0,1:T(8,128)(2,1)S(1)}, u32[]{:S(2)}, u32[]{:S(2)}) async-start(bf16[128,32,128]{2,0,1:T(8,128)(2,1)} %bitcast.17), calls=%async_computation.3 | async-start | bytes 2097152 | tf_op jit(solution)/shard_map/all_to_all | solution.py:114
  52.7 62.9 %collective-permute-start = (bf16[1,1,128,4096]{3,2,1,0:T(8,128)(2,1)}, bf16[1,1,128,4096]{3,2,1,0:T(8,128)(2,1)S(1)}, u32[]{:S(2)}, u32[]{:S(2)}) collective-permute-start(bf16[1,1,128,4096]{3,2,1,0:T(8,128)(2,1)} %param.10), channel_id=1, source_target_pairs={{0,384},{128,0},{256,128},{384,256},{1,385},{129,1},{257,129},{385... | collective-permute-start | bytes 3145736 | tf_op jit(solution)/shard_map/ppermute | solution.py:16
  116.9 33.2 %all-to-all-start.2 = ((bf16[128,32,128]{0,2,1:T(8,128)(2,1)}), bf16[128,32,128]{0,2,1:T(8,128)(2,1)S(1)}, u32[]{:S(2)}, u32[]{:S(2)}) async-start(bf16[128,32,128]{0,2,1:T(8,128)(2,1)} %bitcast.112), calls=%async_computation.2 | async-start | bytes 2097152 | tf_op jit(solution)/shard_map/all_to_all | solution.py:115
  125.9 31.7 %copy-start.1 = (s32[1,4096]{1,0:T(1,128)S(1)}, s32[1,4096]{1,0:T(1,128)}, u32[]{:S(2)}) copy-start(s32[1,4096]{1,0:T(1,128)} %param.11) | copy-start | bytes 49156
  150.1 33.3 %all-to-all-start = ((bf16[128,32,128]{2,0,1:T(8,128)(2,1)}), bf16[128,32,128]{2,0,1:T(8,128)(2,1)}, u32[]{:S(2)}, u32[]{:S(2)}) async-start(bf16[128,32,128]{2,0,1:T(8,128)(2,1)} %copy.41), calls=%async_computation | async-start | bytes 2097152 | tf_op jit(solution)/shard_map/all_to_all | solution.py:112
  316.6 54.7 %all-to-all-start.5 = ((f32[4096,1,128]{2,1,0:T(1,128)}), f32[4096,1,128]{2,1,0:T(1,128)S(1)}, u32[]{:S(2)}, u32[]{:S(2)}) async-start(f32[4096,1,128]{2,1,0:T(1,128)} %bitcast.108), calls=%async_computation.5 | async-start | bytes 4194304 | tf_op jit(solution)/shard_map/all_to_all | solution.py:137
  428.7 55.4 %all-to-all-start.4 = ((f32[4096,1,128]{2,1,0:T(1,128)}), f32[4096,1,128]{2,1,0:T(1,128)}, u32[]{:S(2)}, u32[]{:S(2)}) async-start(f32[4096,1,128]{2,1,0:T(1,128)} %bitcast.116), calls=%async_computation.4 | async-start | bytes 4194304 | tf_op jit(solution)/shard_map/all_to_all | solution.py:136
  436.7 418.1 %all-gather.3.cloned.1.call-start = ((), (), s32[]{:S(2)}) async-start(), calls=%async_computation.7 | async-start | bytes 2641920 | tf_op jit(solution)/shard_map/all_gather | solution.py:154
Sparse Core Ops, SparseCore 0:
  486.6 368.2 all-gather.2
